TPU v7x, 32 devices: a whole 2x2x4 slice. The times are simulated.
32 devices in a mesh: group: 4 (over y, x), dom: 8 (over z, core).
Axes of the slice: x: 2, y: 2, z: 4, core: 2. Of those that a mesh axis runs over, the one named last changes fastest.
Arguments:
- pin_feats: bfloat16 [32768, 256], P(('group', 'dom')), may hold values from -6 to 6
- w_self: bfloat16 [256, 256], replicated, may hold values from -0.375 to 0.375
- w_edge: bfloat16 [4, 256, 256], replicated, may hold values from -0.375 to 0.375
- w_head: bfloat16 [256, 1024], replicated, may hold values from -0.375 to 0.375
- w_out: bfloat16 [1024], replicated, may hold values from -0.1875 to 0.1875
- send_rows: int32 [32, 512], P(('group', 'dom')), may hold values from 0 to 1023
- edge_src: int32 [32, 4, 1024], P(('group', 'dom')), may hold values from 0 to 1535
- edge_dst: int32 [32, 4, 1024], P(('group', 'dom')), may hold values from 0 to 1023
- pin_owner: int32 [32768, 1], P(('group', 'dom')), may hold values from 0 to 31; in each aligned block of 1024 rows (0 to 1023, 1024 to 2047, ...) at most 64 rows name the same one
- pin_net: int32 [32768], P(('group', 'dom')), may hold values from 0 to 255
- net_target: float32 [8192], P(('group', 'dom')), may hold values from -6 to 6
Outputs:
- prediction: float32 [8192], P(('group', 'dom'))
- grad_feats: bfloat16 [32768, 256], P(('group', 'dom'))
- grad_self: float32 [256, 256], replicated
- grad_edge: float32 [4, 256, 256], replicated
- grad_head: float32 [256, 1024], replicated
- grad_out: float32 [1024], replicated
Inputs may be any that keep to these rules, and one draw needn't show every extreme that they name: `pin_owner`: among the pins of one device at most 64 name one owner, and in every draw some device sends exactly 64 pins to some owner.
All inputs are finite; a program needn't handle non-finite values.
Results may differ from a plain program's by a relative error of at most 0.0094.
Values may be sent and summed in bfloat16 or wider, within the bound.
No kernel may reach another device: no remote copies, remote signals or barrier semaphores. Data moves between devices by JAX's collectives and lax.ppermute only.
A program may use at most 64 MiB of HBM per device.

v0:
```python
import math
import jax
import jax.numpy as jnp
from jax import lax
from jax.sharding import PartitionSpec as P

F32 = jnp.float32
BF16 = jnp.bfloat16


def extended(block, sides, width):
    for axis, dim in sides:
        count = lax.axis_size(axis)
        forward = [(i, i + 1) for i in range(count - 1)]
        backward = [(target, source) for source, target in forward]
        low = lax.ppermute(
            lax.slice_in_dim(block, block.shape[dim] - width, None, axis=dim), axis, forward
        )
        high = lax.ppermute(lax.slice_in_dim(block, 0, width, axis=dim), axis, backward)
        block = jnp.concatenate([low, block, high], axis=dim)
    return block


def silu_slope(values):
    sigma_val = jax.nn.sigmoid(values)
    return sigma_val * (1.0 + values * (1.0 - sigma_val))


def one_hot(index, count):
    return (index[..., None] == jnp.arange(count, dtype=index.dtype)).astype(BF16)


def split_dot(spec, left, right):
    return jnp.einsum(
        spec, left, right.astype(F32), precision=lax.Precision.HIGHEST, preferred_element_type=F32
    )


def on_device(
    pin_feats,
    w_self,
    w_edge,
    w_head,
    w_out,
    send_rows,
    edge_src,
    edge_dst,
    pin_owner,
    pin_net,
    net_target,
):
    pin_count, feat_width = pin_feats.shape
    send_list = send_rows[0]
    halo_span = send_list.shape[0] // 2
    send_hot = one_hot(send_list, pin_count)
    outgoing = jnp.dot(send_hot, pin_feats, preferred_element_type=F32).astype(BF16)
    padded = extended(outgoing, (("dom", 0),), halo_span)
    node_table = jnp.concatenate([pin_feats, padded[:halo_span], padded[3 * halo_span :]], 0)
    table_rows = node_table.shape[0]
    sources = edge_src[0]
    endpoints = edge_dst[0]
    src_hot = one_hot(sources, table_rows)
    dst_hot = one_hot(endpoints, pin_count)
    gathered = jnp.einsum("ter,rd->ted", src_hot, node_table, preferred_element_type=F32).astype(
        BF16
    )
    edge_in = jnp.einsum("tep,ted->tpd", dst_hot, gathered, preferred_element_type=F32)
    summed = split_dot("tpk,tkd->pd", edge_in, w_edge)
    degree = jnp.sum(dst_hot.astype(F32), axis=(0, 1))
    inverse = 1.0 / (1.0 + degree)
    preact = jnp.dot(pin_feats, w_self, preferred_element_type=F32) + summed * inverse[:, None]
    hidden = jax.nn.silu(preact).astype(BF16)
    groups = lax.axis_size("group")
    domains = lax.axis_size("dom")
    owners = groups * domains
    capacity = max(2, 2 * pin_count // owners)
    net_count = net_target.shape[0]
    owner_ids = pin_owner[:, 0]
    owner_hot = one_hot(owner_ids, owners)
    earlier = (
        jnp.arange(pin_count, dtype=jnp.int32)[None, :]
        < jnp.arange(pin_count, dtype=jnp.int32)[:, None]
    ).astype(BF16)
    before = jnp.dot(earlier, owner_hot, preferred_element_type=F32)
    slot_rank = jnp.sum(before * owner_hot.astype(F32), axis=1).astype(jnp.int32)
    pin_slot = owner_ids * capacity + slot_rank
    slot_hot = one_hot(pin_slot, owners * capacity)
    net_code = (pin_net + 1).astype(BF16)[:, None]
    slot_nets = (
        jnp.dot(slot_hot.T, net_code, preferred_element_type=F32)[:, 0].astype(jnp.int32) - 1
    )
    slot_nets_in = lax.all_to_all(
        slot_nets.reshape(owners, capacity),
        ("group", "dom"),
        split_axis=0,
        concat_axis=0,
        tiled=True,
    ).reshape(-1)
    outbound = jnp.dot(slot_hot.T, hidden, preferred_element_type=F32).astype(BF16)
    inbound = lax.all_to_all(
        outbound.reshape(owners, capacity, feat_width),
        ("group", "dom"),
        split_axis=0,
        concat_axis=0,
        tiled=True,
    ).reshape(-1, feat_width)
    net_hot = one_hot(slot_nets_in, net_count)
    pooled = jnp.einsum("sn,sd->nd", net_hot, inbound, preferred_element_type=F32)
    pooled_b = pooled.astype(BF16)
    head_pre = jnp.dot(pooled_b, w_head, preferred_element_type=F32)
    activated = jax.nn.silu(head_pre).astype(BF16)
    predicted = jnp.dot(activated, w_out, preferred_element_type=F32)
    misfit = predicted - net_target
    head_grad = (misfit[:, None] * w_out.astype(F32)[None, :] * silu_slope(head_pre)).astype(BF16)
    head_sum = jnp.einsum("nd,nh->dh", pooled_b, head_grad, preferred_element_type=F32)
    out_sum = jnp.dot(misfit, activated.astype(F32), precision=lax.Precision.HIGHEST)
    head_totals = lax.psum(jnp.concatenate([head_sum, out_sum[None, :]], 0), ("group", "dom"))
    net_grad = jnp.einsum("nh,dh->nd", head_grad, w_head, preferred_element_type=F32).astype(BF16)
    returned = jnp.dot(net_hot, net_grad, preferred_element_type=F32).astype(BF16)
    arrived = lax.all_to_all(
        returned.reshape(owners, capacity, feat_width),
        ("group", "dom"),
        split_axis=0,
        concat_axis=0,
        tiled=True,
    ).reshape(-1, feat_width)
    pin_grad = jnp.dot(slot_hot, arrived, preferred_element_type=F32)
    preact_grad = (pin_grad * silu_slope(preact)).astype(BF16)
    self_sum = jnp.einsum("pk,pd->kd", pin_feats, preact_grad, preferred_element_type=F32)
    agg_grad = (preact_grad.astype(F32) * inverse[:, None]).astype(BF16)
    edge_rows = jnp.einsum("tep,pd->ted", dst_hot, agg_grad, preferred_element_type=F32).astype(
        BF16
    )
    edge_sum = jnp.einsum("tek,ted->tkd", gathered, edge_rows, preferred_element_type=F32)
    row_in = jnp.einsum("ter,ted->trd", src_hot, edge_rows, preferred_element_type=F32)
    table_grad = split_dot("trd,tkd->rk", row_in, w_edge)
    local_grad = (
        jnp.einsum("pd,kd->pk", preact_grad, w_self, preferred_element_type=F32)
        + table_grad[:pin_count]
    )
    halo_grad = table_grad[pin_count:].astype(BF16)
    back_padded = extended(halo_grad, (("dom", 0),), halo_span)
    received = jnp.concatenate([back_padded[:halo_span], back_padded[3 * halo_span :]], 0)
    grad_feats = (
        local_grad + jnp.einsum("sp,sd->pd", send_hot, received, preferred_element_type=F32)
    ).astype(BF16)
    self_sum, edge_sum, head_totals = lax.optimization_barrier((self_sum, edge_sum, head_totals))
    tail_totals = lax.psum((self_sum, edge_sum), ("group", "dom"))
    grad_scale = 1.0 / math.sqrt(pin_count * owners)
    return (
        predicted,
        grad_feats,
        tail_totals[0] * grad_scale,
        tail_totals[1] * grad_scale,
        head_totals[:feat_width] * grad_scale,
        head_totals[feat_width] * grad_scale,
    )


def solution(mesh):
    in_specs = (
        P(("group", "dom"), None),
        P(),
        P(),
        P(),
        P(),
        P(("group", "dom"), None),
        P(("group", "dom"), None, None),
        P(("group", "dom"), None, None),
        P(("group", "dom"), None),
        P(("group", "dom")),
        P(("group", "dom")),
    )
    out_specs = (P(("group", "dom")), P(("group", "dom"), None), P(), P(), P(), P())
    return jax.shard_map(
        on_device, mesh=mesh, in_specs=in_specs, out_specs=out_specs, check_vma=False
    )
```

profile of v0, /device:TPU:0, one launch (start us, length us, event | category | flops | bytes accessed | tf_op | source)
XLA Modules:
  0.0 383.9 jit_solution(4948331850442410509)
XLA Ops:
  7.9 1.3 fusion.31
  10.0 1.5 fusion.11
  12.2 7.3 %all-to-all-start = ((s32[32,1,64]{2,1,0:T(1,128)}), s32[32,1,64]{2,1,0:T(1,128)S(1)}, u32[]{:S(2)}, u32[]{:S(2)}) async-start(s32[32,1,64]{2,1,0:T(1,128)} %sub.16), calls=%async_computation | async-start | bytes 32768 | tf_op jit(solution)/shard_map/all_to_all | solution.py:92
  20.1 2.2 collective-permute-start
  22.2 1.3 collective-permute-start.1
  23.5 1.9 convert_reduce_fusion
  26.6 4.8 %fusion.20 = bf16[4,1024,256]{2,1,0:T(8,128)(2,1)S(1)} fusion(s32[4,1024]{1,0:T(4,128)S(1)} %bitcast.74, bf16[256,256]{1,0:T(8,128)(2,1)S(1)} %collective-permute-done.1, bf16[256,256]{1,0:T(8,128)(2,1)S(1)} %collective-permute-done, bf16[1024,256]{1,0:T(8,128)(2,1)S(1)} %copy-done.2), kind=kOutput, calls=%fused_computation.29 | convolution fusion | flops 3230924800 | bytes 2899968 | tf_op jit(solution)/shard_map/ter,rd->ted/dot_general | solution.py:64
  31.5 5.8 %fusion.4 = f32[4,1024,256]{2,1,0:T(8,128)S(1)} fusion(bf16[4,1024,256]{2,1,0:T(8,128)(2,1)S(1)} %fusion.20, s32[4,1024]{1,0:T(4,128)S(1)} %bitcast.72), kind=kOutput, calls=%fused_computation.7 | convolution fusion | flops 2151677952 | bytes 6307840 | tf_op jit(solution)/shard_map/tep,ted->tpd/dot_general | solution.py:67
  37.2 2.1 fusion.24
  40.3 3.5 fusion.16
  43.8 7.9 %all-to-all-start.1 = ((bf16[32,64,256]{2,1,0:T(8,128)(2,1)}), bf16[32,64,256]{2,1,0:T(8,128)(2,1)}, u32[]{:S(2)}, u32[]{:S(2)}) async-start(bf16[32,64,256]{2,1,0:T(8,128)(2,1)} %bitcast.60), calls=%async_computation.1 | async-start | bytes 2097152 | tf_op jit(solution)/shard_map/all_to_all | solution.py:100
  53.0 26.2 %all-to-all-done.1 = bf16[32,64,256]{2,1,0:T(8,128)(2,1)} async-done(((bf16[32,64,256]{2,1,0:T(8,128)(2,1)}), bf16[32,64,256]{2,1,0:T(8,128)(2,1)}, u32[]{:S(2)}, u32[]{:S(2)}) %all-to-all-start.1) | async-done | bytes 1048608 | tf_op jit(solution)/shard_map/all_to_all | solution.py:100
  79.3 2.3 fusion.29
  84.3 3.0 convolution_convert_fusion
  87.3 3.4 all-to-all-start.2
  90.8 1.4 fusion.59
  92.1 1.4 fusion.58
  93.5 1.2 pad_maximum_fusion
  94.8 26.5 %all-to-all-done.2 = bf16[32,64,256]{2,1,0:T(8,128)(2,1)} async-done(((bf16[32,64,256]{2,1,0:T(8,128)(2,1)}), bf16[32,64,256]{2,1,0:T(8,128)(2,1)}, u32[]{:S(2)}, u32[]{:S(2)}) %all-to-all-start.2) | async-done | bytes 1048608 | tf_op jit(solution)/shard_map/all_to_all | solution.py:120
  121.2 3.3 fusion.26
  124.6 3.3 fusion.21
  127.9 9.3 %fusion = f32[4,1536,256]{2,1,0:T(8,128)} fusion(bf16[4,1024,256]{2,1,0:T(8,128)(2,1)S(1)} %fusion.21, s32[4,1024]{1,0:T(4,128)S(1)} %bitcast.75), kind=kOutput, calls=%fused_computation.1 | convolution fusion | flops 3227516928 | bytes 8404992 | tf_op jit(solution)/shard_map/ter,ted->trd/dot_general | solution.py:135
  138.3 1.9 fusion.57
  140.2 89.8 %all-reduce.4.cloned.1.call-done = f32[257,1024]{1,0:T(8,128)} async-done(((f32[257,1024]{1,0:T(8,128)}), f32[257,1024]{1,0:T(8,128)}) %all-reduce.4.cloned.1.call-update) | async-done | bytes 1052688 | tf_op jit(solution)/shard_map/psum | solution.py:117
  229.9 5.1 %fusion.54 = (bf16[1536,256]{1,0:T(8,128)(2,1)S(1)}, f32[1536,256]{1,0:T(8,128)S(1)}) fusion(f32[4,1536,256]{2,1,0:T(8,128)} %fusion, bf16[4,256,256]{2,1,0:T(8,128)(2,1)S(1)} %copy-done.1), kind=kOutput, calls=%fused_computation.83 | convolution fusion | flops 4832231424 | bytes 9175040 | tf_op jit(solution)/shard_map/trd,tkd->rk/dot_general | solution.py:34
  235.1 2.1 collective-permute-start.2
  237.2 1.3 collective-permute-start.3
  238.9 2.3 slice_multiply_fusion
  241.2 1.4 slice_multiply_fusion.1
  242.6 1.6 fusion.27
  244.2 128.8 %all-reduce.6.cloned.1.call-done = (f32[256,256]{0,1:T(8,128)}, f32[4,256,256]{2,1,0:T(8,128)}) async-done(((f32[256,256]{0,1:T(8,128)}, f32[4,256,256]{2,1,0:T(8,128)}), (f32[256,256]{0,1:T(8,128)}, f32[4,256,256]{2,1,0:T(8,128)})) %all-reduce.6.cloned.1.call-update) | async-done | bytes 1310736 | tf_op jit(solution)/shard_map/psum | solution.py:148
  374.8 2.3 broadcast_multiply_fusion
  (63 shorter events, 12.1 us)
Async XLA Ops:
  7.2 74.4 %copy-start = (bf16[256,1024]{1,0:T(8,128)(2,1)S(1)}, bf16[256,1024]{1,0:T(8,128)(2,1)}, u32[]{:S(2)}) copy-start(bf16[256,1024]{1,0:T(8,128)(2,1)} %param.14) | copy-start | bytes 1572868
  9.2 10.3 %copy-start.2 = (bf16[1024,256]{1,0:T(8,128)(2,1)S(1)}, bf16[1024,256]{1,0:T(8,128)(2,1)}, u32[]{:S(2)}) copy-start(bf16[1024,256]{1,0:T(8,128)(2,1)} %param.11) | copy-start | bytes 1572868
  9.3 10.3 %copy-start.14 = (s32[1,512]{1,0:T(1,128)S(1)}, s32[1,512]{1,0:T(1,128)}, u32[]{:S(2)}) copy-start(s32[1,512]{1,0:T(1,128)} %param.16) | copy-start | bytes 6148
  10.0 13.5 %copy-start.12 = (s32[1,4,1024]{2,1,0:T(4,128)S(1)}, s32[1,4,1024]{2,1,0:T(4,128)}, u32[]{:S(2)}) copy-start(s32[1,4,1024]{2,1,0:T(4,128)} %param.18) | copy-start | bytes 49156
  10.0 15.5 %copy-start.8 = (bf16[256,256]{1,0:T(8,128)(2,1)S(1)}, bf16[256,256]{1,0:T(8,128)(2,1)}, u32[]{:S(2)}) copy-start(bf16[256,256]{1,0:T(8,128)(2,1)} %param.12) | copy-start | bytes 393220
  11.5 15.1 %copy-start.13 = (s32[1,4,1024]{2,1,0:T(4,128)S(1)}, s32[1,4,1024]{2,1,0:T(4,128)}, u32[]{:S(2)}) copy-start(s32[1,4,1024]{2,1,0:T(4,128)} %param.17) | copy-start | bytes 49156
  12.2 31.6 %all-to-all-start = ((s32[32,1,64]{2,1,0:T(1,128)}), s32[32,1,64]{2,1,0:T(1,128)S(1)}, u32[]{:S(2)}, u32[]{:S(2)}) async-start(s32[32,1,64]{2,1,0:T(1,128)} %sub.16), calls=%async_computation | async-start | bytes 32768 | tf_op jit(solution)/shard_map/all_to_all | solution.py:92
  20.1 5.8 %collective-permute-start = (bf16[256,256]{1,0:T(8,128)(2,1)S(1)}, bf16[256,256]{1,0:T(8,128)(2,1)S(1)}, u32[]{:S(2)}, u32[]{:S(2)}) collective-permute-start(bf16[256,256]{1,0:T(8,128)(2,1)S(1)} %get-tuple-element.22), channel_id=1, source_target_pairs={{0,1},{1,2},{2,3},{3,4},{4,5},{5,6},{6,7},{8,9},{9,10},{10,11},{11... | collective-permute-start | bytes 393224 | tf_op jit(solution)/shard_map/ppermute | solution.py:16
  22.2 4.4 %collective-permute-start.1 = (bf16[256,256]{1,0:T(8,128)(2,1)S(1)}, bf16[256,256]{1,0:T(8,128)(2,1)S(1)}, u32[]{:S(2)}, u32[]{:S(2)}) collective-permute-start(bf16[256,256]{1,0:T(8,128)(2,1)S(1)} %get-tuple-element.23), channel_id=1, source_target_pairs={{1,0},{2,1},{3,2},{4,3},{5,4},{6,5},{7,6},{9,8},{10,9},{11,10},{12... | collective-permute-start | bytes 393224 | tf_op jit(solution)/shard_map/ppermute | solution.py:19
  31.5 5.8 %copy-start.1 = (bf16[4,256,256]{2,1,0:T(8,128)(2,1)S(1)}, bf16[4,256,256]{2,1,0:T(8,128)(2,1)}, u32[]{:S(2)}) copy-start(bf16[4,256,256]{2,1,0:T(8,128)(2,1)} %param.13) | copy-start | bytes 1572868
  39.3 1.0 copy-start.7
  43.8 7.9 %copy-start.9 = (bf16[1024]{0:T(1024)(128)(2,1)S(1)}, bf16[1024]{0:T(1024)(128)(2,1)}, u32[]{:S(2)}) copy-start(bf16[1024]{0:T(1024)(128)(2,1)} %param.15) | copy-start | bytes 6148
  43.8 35.5 %all-to-all-start.1 = ((bf16[32,64,256]{2,1,0:T(8,128)(2,1)}), bf16[32,64,256]{2,1,0:T(8,128)(2,1)}, u32[]{:S(2)}, u32[]{:S(2)}) async-start(bf16[32,64,256]{2,1,0:T(8,128)(2,1)} %bitcast.60), calls=%async_computation.1 | async-start | bytes 2097152 | tf_op jit(solution)/shard_map/all_to_all | solution.py:100
  81.6 1.5 copy-start.11
  82.0 0.8 copy-start.4
  83.1 4.2 %copy-start.10 = (f32[1,256]{1,0:T(1,128)}, f32[1,256]{1,0:T(1,128)S(1)}, u32[]{:S(2)}) copy-start(f32[1,256]{1,0:T(1,128)S(1)} %fusion.56) | copy-start | bytes 3076
  87.3 33.9 %all-to-all-start.2 = ((bf16[32,64,256]{2,1,0:T(8,128)(2,1)}), bf16[32,64,256]{2,1,0:T(8,128)(2,1)}, u32[]{:S(2)}, u32[]{:S(2)}) async-start(bf16[32,64,256]{2,1,0:T(8,128)(2,1)} %bitcast.59), calls=%async_computation.2 | async-start | bytes 2097152 | tf_op jit(solution)/shard_map/all_to_all | solution.py:120
  90.7 139.2 %all-reduce.4.cloned.1.call-start = ((), (), s32[]{:S(2)}) async-start(), calls=%async_computation.3 | async-start | bytes 2162688 | tf_op jit(solution)/shard_map/psum | solution.py:117
  94.7 278.2 %all-reduce.6.cloned.1.call-start = ((), (), s32[]{:S(2)}) async-start(), calls=%async_computation.4 | async-start | bytes 2621440 | tf_op jit(solution)/shard_map/psum | solution.py:148
  124.6 12.7 %copy-start.5 = (bf16[1024,256]{1,0:T(8,128)(2,1)}, bf16[1024,256]{1,0:T(8,128)(2,1)S(1)}, u32[]{:S(2)}) copy-start(bf16[1024,256]{1,0:T(8,128)(2,1)S(1)} %fusion.26) | copy-start | bytes 1572868
  127.9 9.4 %copy-start.3 = (bf16[1024,256]{1,0:T(8,128)(2,1)S(1)}, bf16[1024,256]{1,0:T(8,128)(2,1)}, u32[]{:S(2)}) copy-start(bf16[1024,256]{1,0:T(8,128)(2,1)} %param.11) | copy-start | bytes 1572868
  140.2 98.3 %copy-start.6 = (bf16[1024,256]{1,0:T(8,128)(2,1)S(1)}, bf16[1024,256]{1,0:T(8,128)(2,1)}, u32[]{:S(2)}) copy-start(bf16[1024,256]{1,0:T(8,128)(2,1)} %copy-done.5) | copy-start | bytes 1572868
  235.1 7.5 %collective-permute-start.2 = (bf16[256,256]{1,0:T(8,128)(2,1)S(1)}, bf16[256,256]{1,0:T(8,128)(2,1)S(1)}, u32[]{:S(2)}, u32[]{:S(2)}) collective-permute-start(bf16[256,256]{1,0:T(8,128)(2,1)S(1)} %get-tuple-element.20), channel_id=1, source_target_pairs={{0,1},{1,2},{2,3},{3,4},{4,5},{5,6},{6,7},{8,9},{9,10},{10,11},{11... | collective-permute-start | bytes 393224 | tf_op jit(solution)/shard_map/ppermute | solution.py:16
  237.2 5.4 %collective-permute-start.3 = (bf16[256,256]{1,0:T(8,128)(2,1)S(1)}, bf16[256,256]{1,0:T(8,128)(2,1)S(1)}, u32[]{:S(2)}, u32[]{:S(2)}) collective-permute-start(bf16[256,256]{1,0:T(8,128)(2,1)S(1)} %get-tuple-element.21), channel_id=1, source_target_pairs={{1,0},{2,1},{3,2},{4,3},{5,4},{6,5},{7,6},{9,8},{10,9},{11,10},{12... | collective-permute-start | bytes 393224 | tf_op jit(solution)/shard_map/ppermute | solution.py:19
Sparse Core Ops, SparseCore 0:
  97.0 132.9 all-reduce.3
  239.0 133.9 all-reduce.5
where the time goes:
time: 385 us; the launch traced here: 384 us
  waiting for transfers between devices  272 us (71%)
  matrix products  54.4 us (14%)
  starting transfers between devices  25.5 us (7%)
  between operations  14.4 us (4%)
  other arithmetic  13.6 us (4%)
  local copies, waits for them, and re-layouts  3.99 us (1%)
    psum x1, waiting for transfers between devices, on_device(): tail_totals = lax.psum((self_sum, edge_sum), ('group', 'dom'))  129 us
    psum x1, waiting for transfers between devices, on_device(): lax.psum(jnp.concatenate([head_sum, out_sum[None, :]], 0), ('group', 'dom'))  89.8 us
    all_to_all x1, waiting for transfers between devices, on_device(): lax.all_to_all(returned.reshape(owners, capacity, feat_width), ('group',...  26.5 us
    all_to_all x1, waiting for transfers between devices, on_device(): lax.all_to_all(outbound.reshape(owners, capacity, feat_width), ('group',...  26.2 us
    dot_general x1, matrix products, on_device(): jnp.einsum('ter,ted->trd', src_hot, edge_rows, preferred_element_type=F32)  9.33 us
    all_to_all x1, starting transfers between devices, on_device(): lax.all_to_all(outbound.reshape(owners, capacity, feat_width), ('group',...  7.91 us
  transfers between devices with their start and end apart: 9, of which 5 were waited for; matrix products, arithmetic and copies ran while one was open for 13% of the time, Pallas kernels for 0%

commit v1 on v0

--- a/solution.py
+++ b/solution.py
@@ -114,7 +114,9 @@
     head_grad = (misfit[:, None] * w_out.astype(F32)[None, :] * silu_slope(head_pre)).astype(BF16)
     head_sum = jnp.einsum("nd,nh->dh", pooled_b, head_grad, preferred_element_type=F32)
     out_sum = jnp.dot(misfit, activated.astype(F32), precision=lax.Precision.HIGHEST)
-    head_totals = lax.psum(jnp.concatenate([head_sum, out_sum[None, :]], 0), ("group", "dom"))
+    head_totals = jnp.sum(
+        lax.all_gather(jnp.concatenate([head_sum, out_sum[None, :]], 0), ("group", "dom")), axis=0
+    )
     net_grad = jnp.einsum("nh,dh->nd", head_grad, w_head, preferred_element_type=F32).astype(BF16)
     returned = jnp.dot(net_hot, net_grad, preferred_element_type=F32).astype(BF16)
     arrived = lax.all_to_all(

time: 385 us -> 456 us (1.18)
  blocking collectives: 0 us -> 51.3 us
  waiting for transfers between devices: 272 us -> 292 us
  other arithmetic: 13.6 us -> 21.1 us
  matrix products: 54.4 us -> 49.6 us
    all_gather x0 -> x1, waiting for transfers between devices: none -> 139 us  [on_device(): lax.all_gather(jnp.concatenate([head_sum, out_sum[None, :]], 0), ('group'...]
    psum x1 -> x0, waiting for transfers between devices: 89.8 us -> none  [on_device(): lax.psum(jnp.concatenate([head_sum, out_sum[None, :]], 0), ('group', 'dom'))]
    all_to_all x0 -> x1, blocking collectives: none -> 51.3 us  [on_device(): lax.all_to_all(returned.reshape(owners, capacity, feat_width), ('group',...]
    all_to_all x1 -> x0, waiting for transfers between devices: 26.5 us -> none  [on_device(): lax.all_to_all(returned.reshape(owners, capacity, feat_width), ('group',...]
    reduce_sum x0 -> x1, other arithmetic: none -> 12 us  [on_device(): jnp.sum(lax.all_gather(jnp.concatenate([head_sum, out_sum[None, :]], 0),...]
  transfers between devices with their start and end apart: 9 -> 8, of which waited for: 5 -> 3; matrix products, arithmetic and copies ran while one was open for 13% -> 14% of each run, Pallas kernels for 0% -> 0%
where the time goes in v1:
time: 456 us; the launch traced here: 455 us
  waiting for transfers between devices  292 us (64%)
  blocking collectives  51.3 us (11%)
  matrix products  49.6 us (11%)
  starting transfers between devices  22.2 us (5%)
  other arithmetic  21.1 us (5%)
  between operations  14.5 us (3%)
  local copies, waits for them, and re-layouts  4.65 us (1%)
    all_gather x1, waiting for transfers between devices, on_device(): lax.all_gather(jnp.concatenate([head_sum, out_sum[None, :]], 0), ('group'...  139 us
    psum x1, waiting for transfers between devices, on_device(): tail_totals = lax.psum((self_sum, edge_sum), ('group', 'dom'))  126 us
    all_to_all x1, blocking collectives, on_device(): lax.all_to_all(returned.reshape(owners, capacity, feat_width), ('group',...  51.3 us
    all_to_all x1, waiting for transfers between devices, on_device(): lax.all_to_all(outbound.reshape(owners, capacity, feat_width), ('group',...  26.2 us
    reduce_sum x1, other arithmetic, on_device(): jnp.sum(lax.all_gather(jnp.concatenate([head_sum, out_sum[None, :]], 0),...  12 us
  transfers between devices with their start and end apart: 8, of which 3 were waited for; matrix products, arithmetic and copies ran while one was open for 14% of the time, Pallas kernels for 0%

profile of v1, /device:TPU:0, one launch (start us, length us, event | category | flops | bytes accessed | tf_op | source)
XLA Modules:
  0.0 455.4 jit_solution(11092118578520581222)
XLA Ops:
  7.2 1.6 fusion.28
  8.9 1.3 collective-permute-start.1
  10.2 3.0 collective-permute-start
  13.9 1.5 fusion.11
  16.0 7.3 %all-to-all-start = ((s32[32,1,64]{2,1,0:T(1,128)}), s32[32,1,64]{2,1,0:T(1,128)S(1)}, u32[]{:S(2)}, u32[]{:S(2)}) async-start(s32[32,1,64]{2,1,0:T(1,128)} %sub.16), calls=%async_computation | async-start | bytes 32768 | tf_op jit(solution)/shard_map/all_to_all | solution.py:92
  23.7 1.9 convert_reduce_fusion
  26.3 5.7 %fusion.20 = bf16[4,1024,256]{2,1,0:T(8,128)(2,1)S(1)} fusion(s32[4,1024]{1,0:T(4,128)S(1)} %bitcast.77, bf16[256,256]{1,0:T(8,128)(2,1)S(1)} %collective-permute-done.1, bf16[256,256]{1,0:T(8,128)(2,1)} %copy-done.15, bf16[1024,256]{1,0:T(8,128)(2,1)S(1)} %copy-done.3), kind=kOutput, calls=%fused_computation.29 | convolution fusion | flops 3230924800 | bytes 2899968 | tf_op jit(solution)/shard_map/ter,rd->ted/dot_general | solution.py:64
  32.1 5.8 %fusion.4 = f32[4,1024,256]{2,1,0:T(8,128)S(1)} fusion(bf16[4,1024,256]{2,1,0:T(8,128)(2,1)S(1)} %fusion.20, s32[4,1024]{1,0:T(4,128)S(1)} %bitcast.75), kind=kOutput, calls=%fused_computation.7 | convolution fusion | flops 2151677952 | bytes 6307840 | tf_op jit(solution)/shard_map/tep,ted->tpd/dot_general | solution.py:67
  37.8 2.1 fusion.24
  40.9 3.5 fusion.16
  44.4 6.0 %all-to-all-start.1 = ((bf16[32,64,256]{2,1,0:T(8,128)(2,1)}), bf16[32,64,256]{2,1,0:T(8,128)(2,1)}, u32[]{:S(2)}, u32[]{:S(2)}) async-start(bf16[32,64,256]{2,1,0:T(8,128)(2,1)} %bitcast.61), calls=%async_computation.1 | async-start | bytes 2097152 | tf_op jit(solution)/shard_map/all_to_all | solution.py:100
  51.8 26.2 %all-to-all-done.1 = bf16[32,64,256]{2,1,0:T(8,128)(2,1)} async-done(((bf16[32,64,256]{2,1,0:T(8,128)(2,1)}), bf16[32,64,256]{2,1,0:T(8,128)(2,1)}, u32[]{:S(2)}, u32[]{:S(2)}) %all-to-all-start.1) | async-done | bytes 1048608 | tf_op jit(solution)/shard_map/all_to_all | solution.py:100
  78.0 2.3 fusion.29
  82.8 1.1 maximum_bitcast_fusion
  84.0 3.0 convolution_convert_fusion
  87.0 51.3 %all_to_all.16 = bf16[32,64,256]{2,1,0:T(8,128)(2,1)S(1)} all-to-all(bf16[32,64,256]{2,1,0:T(8,128)(2,1)} %bitcast.63), channel_id=1, replica_groups=mesh['group'=4,'dom'=8] {'group','dom'}, dimensions={0} | all-to-all | bytes 2097152 | tf_op jit(solution)/shard_map/all_to_all | solution.py:122
  138.3 1.8 fusion.26
  140.1 3.3 fusion.21
  143.4 8.0 %fusion = f32[4,1536,256]{2,1,0:T(8,128)S(1)} fusion(bf16[4,1024,256]{2,1,0:T(8,128)(2,1)S(1)} %fusion.21, s32[4,1024]{1,0:T(4,128)S(1)} %bitcast.78), kind=kOutput, calls=%fused_computation.1 | convolution fusion | flops 3227516928 | bytes 8404992 | tf_op jit(solution)/shard_map/ter,ted->trd/dot_general | solution.py:137
  151.3 3.1 fusion.54
  154.5 1.3 collective-permute-start.3
  155.8 3.3 collective-permute-start.2
  159.1 1.3 convolution_add_fusion
  160.4 1.9 fusion.57
  162.3 1.0 convolution_bitcast_fusion.2
  163.3 139.3 %all-gather.4.cloned.1.call-done = f32[32,257,1024]{2,1,0:T(8,128)} async-done(((f32[1,257,1024]{2,1,0:T(8,128)}), f32[32,257,1024]{2,1,0:T(8,128)}) %all-gather.4.cloned.1.call-update) | async-done | bytes 33685520 | tf_op jit(solution)/shard_map/all_gather | solution.py:118
  302.6 12.0 %reduce_sum.29 = f32[257,1024]{1,0:T(8,128)S(1)} reduce(f32[32,257,1024]{2,1,0:T(8,128)} %all-gather.4.cloned.1.call-done, f32[]{:T(128)} %constant.7.clone.1), dimensions={0}, to_apply=%region_2.3 | reduce | flops 8158208 | bytes 34738180 | tf_op jit(solution)/shard_map/reduce_sum | solution.py:117
  314.7 1.6 fusion.27
  316.9 1.1 slice_multiply_fusion
  318.0 126.5 %all-reduce.3.cloned.1.call-done = (f32[256,256]{0,1:T(8,128)}, f32[4,256,256]{2,1,0:T(8,128)}) async-done(((f32[256,256]{0,1:T(8,128)}, f32[4,256,256]{2,1,0:T(8,128)}), (f32[256,256]{0,1:T(8,128)}, f32[4,256,256]{2,1,0:T(8,128)})) %all-reduce.3.cloned.1.call-update) | async-done | bytes 1310736 | tf_op jit(solution)/shard_map/psum | solution.py:150
  444.4 1.0 broadcast_multiply_fusion.1
  446.3 2.3 broadcast_multiply_fusion
  (71 shorter events, 8.7 us)
Async XLA Ops:
  7.2 73.1 %copy-start = (bf16[256,1024]{1,0:T(8,128)(2,1)S(1)}, bf16[256,1024]{1,0:T(8,128)(2,1)}, u32[]{:S(2)}) copy-start(bf16[256,1024]{1,0:T(8,128)(2,1)} %param.14) | copy-start | bytes 1572868
  7.2 6.0 %copy-start.12 = (s32[1024,1]{0,1:T(1,128)S(1)}, s32[1024,1]{0,1:T(1,128)}, u32[]{:S(2)}) copy-start(s32[1024,1]{0,1:T(1,128)} %param.19) | copy-start | bytes 12292
  7.2 6.6 %copy-start.13 = (s32[1024]{0:T(1024)S(1)}, s32[1024]{0:T(1024)}, u32[]{:S(2)}) copy-start(s32[1024]{0:T(1024)} %param.20) | copy-start | bytes 12292
  8.9 16.8 %collective-permute-start.1 = (bf16[256,256]{1,0:T(8,128)(2,1)S(1)}, bf16[256,256]{1,0:T(8,128)(2,1)S(1)}, u32[]{:S(2)}, u32[]{:S(2)}) collective-permute-start(bf16[256,256]{1,0:T(8,128)(2,1)S(1)} %get-tuple-element.29), channel_id=1, source_target_pairs={{1,0},{2,1},{3,2},{4,3},{5,4},{6,5},{7,6},{9,8},{10,9},{11,10},{12... | collective-permute-start | bytes 393224 | tf_op jit(solution)/shard_map/ppermute | solution.py:19
  10.2 15.5 %collective-permute-start = (bf16[256,256]{1,0:T(8,128)(2,1)S(1)}, bf16[256,256]{1,0:T(8,128)(2,1)S(1)}, u32[]{:S(2)}, u32[]{:S(2)}) collective-permute-start(bf16[256,256]{1,0:T(8,128)(2,1)S(1)} %get-tuple-element.28), channel_id=1, source_target_pairs={{0,1},{1,2},{2,3},{3,4},{4,5},{5,6},{6,7},{8,9},{9,10},{10,11},{11... | collective-permute-start | bytes 393224 | tf_op jit(solution)/shard_map/ppermute | solution.py:16
  13.8 9.6 %copy-start.3 = (bf16[1024,256]{1,0:T(8,128)(2,1)S(1)}, bf16[1024,256]{1,0:T(8,128)(2,1)}, u32[]{:S(2)}) copy-start(bf16[1024,256]{1,0:T(8,128)(2,1)} %param.11) | copy-start | bytes 1572868
  13.8 9.6 %copy-start.9 = (bf16[256,256]{1,0:T(8,128)(2,1)S(1)}, bf16[256,256]{1,0:T(8,128)(2,1)}, u32[]{:S(2)}) copy-start(bf16[256,256]{1,0:T(8,128)(2,1)} %param.12) | copy-start | bytes 393220
  13.8 9.8 %copy-start.16 = (s32[1,4,1024]{2,1,0:T(4,128)S(1)}, s32[1,4,1024]{2,1,0:T(4,128)}, u32[]{:S(2)}) copy-start(s32[1,4,1024]{2,1,0:T(4,128)} %param.18) | copy-start | bytes 49156
  13.8 12.5 %copy-start.17 = (s32[1,4,1024]{2,1,0:T(4,128)S(1)}, s32[1,4,1024]{2,1,0:T(4,128)}, u32[]{:S(2)}) copy-start(s32[1,4,1024]{2,1,0:T(4,128)} %param.17) | copy-start | bytes 49156
  16.0 28.4 %all-to-all-start = ((s32[32,1,64]{2,1,0:T(1,128)}), s32[32,1,64]{2,1,0:T(1,128)S(1)}, u32[]{:S(2)}, u32[]{:S(2)}) async-start(s32[32,1,64]{2,1,0:T(1,128)} %sub.16), calls=%async_computation | async-start | bytes 32768 | tf_op jit(solution)/shard_map/all_to_all | solution.py:92
  25.6 0.7 copy-start.15
  32.1 5.8 %copy-start.2 = (bf16[4,256,256]{2,1,0:T(8,128)(2,1)S(1)}, bf16[4,256,256]{2,1,0:T(8,128)(2,1)}, u32[]{:S(2)}) copy-start(bf16[4,256,256]{2,1,0:T(8,128)(2,1)} %param.13) | copy-start | bytes 1572868
  39.9 1.0 copy-start.7
  44.4 6.0 %copy-start.10 = (bf16[1024]{0:T(1024)(128)(2,1)S(1)}, bf16[1024]{0:T(1024)(128)(2,1)}, u32[]{:S(2)}) copy-start(bf16[1024]{0:T(1024)(128)(2,1)} %param.15) | copy-start | bytes 6148
  44.4 33.5 %all-to-all-start.1 = ((bf16[32,64,256]{2,1,0:T(8,128)(2,1)}), bf16[32,64,256]{2,1,0:T(8,128)(2,1)}, u32[]{:S(2)}, u32[]{:S(2)}) async-start(bf16[32,64,256]{2,1,0:T(8,128)(2,1)} %bitcast.61), calls=%async_computation.1 | async-start | bytes 2097152 | tf_op jit(solution)/shard_map/all_to_all | solution.py:100
  50.4 252.2 %all-gather.4.cloned.1.call-start = ((), (), s32[]{:S(2)}) async-start(), calls=%async_computation.3 | async-start | bytes 35684352 | tf_op jit(solution)/shard_map/all_gather | solution.py:118
  80.2 0.7 copy-start.14
  80.9 3.0 copy-start.11
  81.7 0.8 copy-start.5
  84.0 360.5 %all-reduce.3.cloned.1.call-start = ((), (), s32[]{:S(2)}) async-start(), calls=%async_computation.4 | async-start | bytes 2621440 | tf_op jit(solution)/shard_map/psum | solution.py:150
  87.0 51.3 %copy-start.8 = (f32[1024,256]{1,0:T(8,128)S(1)}, f32[1024,256]{1,0:T(8,128)}, u32[]{:S(2)}) copy-start(f32[1024,256]{1,0:T(8,128)} %copy-done.7) | copy-start | bytes 3145732
  154.5 160.1 %collective-permute-start.3 = (bf16[256,256]{1,0:T(8,128)(2,1)S(1)}, bf16[256,256]{1,0:T(8,128)(2,1)S(1)}, u32[]{:S(2)}, u32[]{:S(2)}) collective-permute-start(bf16[256,256]{1,0:T(8,128)(2,1)S(1)} %get-tuple-element.27), channel_id=1, source_target_pairs={{1,0},{2,1},{3,2},{4,3},{5,4},{6,5},{7,6},{9,8},{10,9},{11,10},{12... | collective-permute-start | bytes 393224 | tf_op jit(solution)/shard_map/ppermute | solution.py:19
  155.8 158.9 %collective-permute-start.2 = (bf16[256,256]{1,0:T(8,128)(2,1)S(1)}, bf16[256,256]{1,0:T(8,128)(2,1)S(1)}, u32[]{:S(2)}, u32[]{:S(2)}) collective-permute-start(bf16[256,256]{1,0:T(8,128)(2,1)S(1)} %get-tuple-element.26), channel_id=1, source_target_pairs={{0,1},{1,2},{2,3},{3,4},{4,5},{5,6},{6,7},{8,9},{9,10},{10,11},{11... | collective-permute-start | bytes 393224 | tf_op jit(solution)/shard_map/ppermute | solution.py:16
  160.4 1.9 copy-start.4
  163.3 151.4 %copy-start.6 = (f32[1024,256]{1,0:T(8,128)S(1)}, f32[1024,256]{1,0:T(8,128)}, u32[]{:S(2)}) copy-start(f32[1024,256]{1,0:T(8,128)} %convolution_add_fusion) | copy-start | bytes 3145732
  163.3 151.4 %copy-start.18 = (s32[1,512]{1,0:T(1,128)S(1)}, s32[1,512]{1,0:T(1,128)}, u32[]{:S(2)}) copy-start(s32[1,512]{1,0:T(1,128)} %param.16) | copy-start | bytes 6148
  316.9 131.7 %copy-start.1 = (bf16[256,1024]{1,0:T(8,128)(2,1)S(1)}, bf16[256,1024]{1,0:T(8,128)(2,1)}, u32[]{:S(2)}) copy-start(bf16[256,1024]{1,0:T(8,128)(2,1)} %param.14) | copy-start | bytes 1572868
Sparse Core Ops, SparseCore 0:
  84.1 218.5 all-gather.3
  314.7 129.6 all-reduce.2
